TPU v7x, 512 devices: a whole 4x8x8 slice. The times are simulated.
512 devices in a mesh: sub: 128 (over z_hi, x, y, core), scen: 4 (over z_lo).
Axes of the slice: x: 4, y: 8, z: 8 (z_hi: 2, z_lo: 4; z = z_hi * 4 + z_lo), core: 2. Of those that a mesh axis runs over, the one named last changes fastest.
Arguments:
- inverse_matrix: bfloat16 [128, 1024, 1024], P('sub'), may hold values from -1 to 1
- objective_grad: bfloat16 [48, 128, 64, 1024], P(None, 'sub', 'scen'), may hold values from -6 to 6
- final_adjoint: float32 [128, 64, 1024], P('sub', 'scen'), may hold values from -6 to 6
- companion: float32 [128, 1024], P('sub'), may hold values from 0.95 to 0.995
- port_node: int32 [128, 4, 8], P('sub'), may hold values from 0 to 1023
- line_count: int32 [128, 4], P('sub'), may hold values from 1 to 8, as said below
- line_delay: int32 [128, 4, 8], P('sub'), may hold values from 24 to 47, as said below
- line_admittance: float32 [128, 4, 8], P('sub'), may hold values from 0.3 to 1.2
- later_history: float32 [128, 4, 8, 48, 64], P('sub', None, None, None, 'scen'), may hold values from -6 to 6
- conv_node: int32 [128, 16], P('sub'), may hold values from 0 to 1023
- conv_drive: float32 [128, 48, 64, 16], P('sub', None, 'scen'), may hold values from -0.25 to 0.25
- fault_bus: int32 [64], P('scen'), may hold values from 0 to 131071
- fault_current: float32 [48, 64], P(None, 'scen'), may hold values from -12 to 12
- fault_voltage: float32 [48, 64], P(None, 'scen'), may hold values from -2 to 2
Outputs:
- adjoint_start: float32 [128, 64, 1024], P('sub', 'scen')
- earlier_history: float32 [128, 4, 8, 48, 64], P('sub', None, None, None, 'scen')
- control_sens: float32 [128, 16], P('sub')
- fault_sens: float32 [64], P('scen')
Inputs may be any that keep to these rules, and one draw needn't show every extreme that they name: line_count[p, e] equals line_count of the partner subnetwork in the opposite direction; the most is reached in every draw. `line_delay`: both ends of a line have the same delay; both ends of the range are reached in every draw.
All inputs are finite; a program needn't handle non-finite values.
Results may differ from a plain program's by a relative error of at most 0.0088.
Values sent between devices are 32-bit elements; how exact they have to be, the bound alone decides.
No kernel may reach another device: no remote copies, remote signals or barrier semaphores. Data moves between devices by JAX's collectives and lax.ppermute only.
A program may use at most 64 MiB of HBM per device.

v0:
```python
import jax
import jax.numpy as jnp
from jax import lax
from jax.sharding import PartitionSpec as P

PRECISE = lax.Precision.HIGHEST


def passed_along(value, axis, steps):
    count = lax.axis_size(axis)
    pairs = [(source, (source + steps) % count) for source in range(count)]
    return lax.ppermute(value, axis, pairs)


def body(
    inverse_matrix,
    objective_grad,
    final_adjoint,
    companion,
    port_node,
    line_count,
    line_delay,
    line_admittance,
    later_history,
    conv_node,
    conv_drive,
    fault_bus,
    fault_current,
    fault_voltage,
):
    node_count = inverse_matrix.shape[1]
    scen_rows = objective_grad.shape[2]
    slot_count = port_node.shape[2]
    port_total = 4 * slot_count
    conv_count = conv_node.shape[1]
    block_len = later_history.shape[3] // 2
    blocks = objective_grad.shape[0] // block_len
    sub_count = lax.axis_size("sub")
    grid_width = max(2, sub_count // 16)
    offsets = (1, -1, grid_width, -grid_width)
    opposite = (1, 0, 3, 2)
    sub_index = lax.axis_index("sub")
    weights = inverse_matrix[0]
    live_mask = (lax.iota(jnp.int32, slot_count)[None, :] < line_count[0][:, None]).astype(
        jnp.float32
    )
    node_iota = lax.iota(jnp.int32, node_count)
    pick_table = jnp.concatenate(
        [
            node_iota[:, None] == port_node[0].reshape(port_total)[None, :],
            node_iota[:, None] == conv_node[0][None, :],
        ],
        axis=1,
    ).astype(jnp.float32)
    spread_table = jnp.transpose(pick_table[:, :port_total])
    line_scale = (line_admittance[0] * live_mask).reshape(port_total)
    fault_table = (node_iota[None, :] == (fault_bus - sub_index * node_count)[:, None]).astype(
        jnp.float32
    )
    window = later_history[0]
    adjoint_next = final_adjoint[0]
    control_local = jnp.zeros((conv_count,), jnp.float32)
    fault_local = jnp.zeros((scen_rows,), jnp.float32)
    block_rows = lax.iota(jnp.int32, block_len)
    time_iota = lax.iota(jnp.int32, 2 * block_len)

    def one_step(adjoint_prev, inputs):
        grad_now, inflow_now, current_now = inputs
        right_side = (
            grad_now.astype(jnp.float32)
            + companion[0][None, :] * adjoint_prev
            + inflow_now
            + current_now[:, None] * fault_table
        )
        adjoint = jnp.dot(
            right_side.astype(jnp.bfloat16), weights, preferred_element_type=jnp.float32
        )
        return (adjoint, adjoint)

    for block_id in reversed(range(blocks)):
        block_start = block_id * block_len
        target = block_rows[None, None, :] + line_delay[0][:, :, None] - block_len
        time_table = (target[..., None] == time_iota).astype(jnp.float32)
        picked = (
            jnp.einsum("ecji,ecis->jsec", time_table, window, precision=PRECISE).reshape(
                block_len * scen_rows, port_total
            )
            * line_scale[None, :]
        )
        inflow = jnp.dot(picked, spread_table, precision=PRECISE).reshape(
            block_len, scen_rows, node_count
        )
        adjoint_next, adjoint_block = lax.scan(
            one_step,
            adjoint_next,
            (
                objective_grad[block_start : block_start + block_len, 0],
                inflow,
                fault_current[block_start : block_start + block_len],
            ),
            reverse=True,
        )
        samples = jnp.dot(
            adjoint_block.reshape(block_len * scen_rows, node_count), pick_table, precision=PRECISE
        )
        series = (
            jnp.transpose(
                samples[:, :port_total].reshape(block_len, scen_rows, 4, slot_count), (2, 3, 0, 1)
            )
            * live_mask[:, :, None, None]
        )
        outbound = series.reshape(4, slot_count, block_len * scen_rows)
        control_term = jnp.sum(
            samples[:, port_total:].reshape(block_len, scen_rows, conv_count)
            * conv_drive[0, block_start : block_start + block_len],
            axis=(0, 1),
        )
        fault_term = jnp.sum(
            jnp.sum(adjoint_block * fault_table[None], axis=2)
            * fault_voltage[block_start : block_start + block_len],
            axis=0,
        )
        control_local = control_local + lax.psum(control_term, "scen")
        fault_local = fault_local + lax.psum(fault_term, "sub")
        received = jnp.stack(
            [
                passed_along(outbound[opposite[direction]], "sub", -offsets[direction])
                for direction in range(4)
            ]
        )
        window = jnp.concatenate(
            [received.reshape(4, slot_count, block_len, scen_rows), window[:, :, :block_len]],
            axis=2,
        )
    return (adjoint_next[None], window[None], control_local[None], fault_local)


def solution(mesh):
    return jax.shard_map(
        body,
        mesh=mesh,
        in_specs=(
            P("sub", None, None),
            P(None, "sub", "scen", None),
            P("sub", "scen", None),
            P("sub", None),
            P("sub", None, None),
            P("sub", None),
            P("sub", None, None),
            P("sub", None, None),
            P("sub", None, None, None, "scen"),
            P("sub", None),
            P("sub", None, "scen", None),
            P("scen"),
            P(None, "scen"),
            P(None, "scen"),
        ),
        out_specs=(
            P("sub", "scen", None),
            P("sub", None, None, None, "scen"),
            P("sub", None),
            P("scen"),
        ),
        check_vma=False,
    )
```

profile of v0, /device:TPU:64, one launch (start us, length us, event | category | flops | bytes accessed | tf_op | source)
XLA Modules:
  0.0 630.8 jit_solution(12138053387449394268)
XLA Ops:
  6.0 2.4 slice_bitcast_fusion
  9.2 2.0 fusion.45
  12.6 46.1 %while.34 = (s32[]{:T(128)}, f32[16,1024]{1,0:T(8,128)S(1)}, f32[24,16,1024]{2,1,0:T(8,128)}, bf16[24,16,1024]{2,1,0:T(8,128)(2,1)}, f32[1,1024]{1,0:T(1,128)S(1...) while((s32[]{:T(128)}, f32[16,1024]{1,0:T(8,128)S(1)}, ...), condition=%wide.region_1.2_spmd.clone, body=%wide.region_0.1_spmd.clone.sunk | while | flops 33685504 | bytes 2528637 | solution.py:93
  12.7 1.9 bitcast_dynamic-update-slice_fusion.4
  14.6 1.9 bitcast_dynamic-update-slice_fusion.4
  22.3 1.9 bitcast_dynamic-update-slice_fusion.4
  26.1 1.9 bitcast_dynamic-update-slice_fusion.4
  28.0 1.9 bitcast_dynamic-update-slice_fusion.4
  45.3 1.9 bitcast_dynamic-update-slice_fusion.4
  53.0 1.9 bitcast_dynamic-update-slice_fusion.4
  54.9 1.9 bitcast_dynamic-update-slice_fusion.4
  58.9 2.3 fusion.57
  63.5 14.5 %collective-permute-start = (f32[8,384]{1,0:T(8,128)}, f32[8,384]{1,0:T(8,128)S(1)}, u32[]{:S(2)}, u32[]{:S(2)}) collective-permute-start(f32[8,384]{1,0:T(8,128)} %squeeze.91), channel_id=1, source_target_pairs={{0,508},{4,0},{8,4},{12,8},{16,12},{20,16},{24,20},{28,24},{32,28}... | collective-permute-start | bytes 36872 | tf_op jit(solution)/shard_map/ppermute | solution.py:12
  78.1 1.9 collective-permute-start.1
  80.8 5.3 collective-permute-start.2
  86.2 4.4 collective-permute-start.3
  98.0 4.7 collective-permute-done.3
  105.3 2.0 fusion.43
  108.7 62.3 %while.35 = (s32[]{:T(128)}, f32[16,1024]{1,0:T(8,128)S(1)}, f32[24,16,1024]{2,1,0:T(8,128)}, bf16[24,16,1024]{2,1,0:T(8,128)(2,1)S(1)}, f32[1,1024]{1,0:T(1,128...) while((s32[]{:T(128)}, f32[16,1024]{1,0:T(8,128)S(1)}, ...), condition=%wide.region_3.4_spmd.clone, body=%wide.region_2.3_spmd.clone.sunk | while | flops 33685504 | bytes 2529533 | solution.py:93
  109.4 1.9 bitcast_dynamic-update-slice_fusion.5
  122.4 1.9 bitcast_dynamic-update-slice_fusion.5
  125.0 1.9 bitcast_dynamic-update-slice_fusion.5
  127.6 1.9 bitcast_dynamic-update-slice_fusion.5
  145.8 1.9 bitcast_dynamic-update-slice_fusion.5
  151.0 1.9 bitcast_dynamic-update-slice_fusion.5
  171.0 2.3 multiply_reduce_fusion
  174.8 13.4 %collective-permute-start.4 = (f32[8,384]{1,0:T(8,128)S(1)}, f32[8,384]{1,0:T(8,128)S(1)}, u32[]{:S(2)}, u32[]{:S(2)}) collective-permute-start(f32[8,384]{1,0:T(8,128)S(1)} %squeeze.95), channel_id=1, source_target_pairs={{0,508},{4,0},{8,4},{12,8},{16,12},{20,16},{24,20},{28,24},{32,28}... | collective-permute-start | bytes 36872 | tf_op jit(solution)/shard_map/ppermute | solution.py:12
  188.3 1.9 collective-permute-start.5
  190.3 1.9 collective-permute-start.6
  192.3 7.8 %collective-permute-start.7 = (f32[8,384]{1,0:T(8,128)S(1)}, f32[8,384]{1,0:T(8,128)S(1)}, u32[]{:S(2)}, u32[]{:S(2)}) collective-permute-start(f32[8,384]{1,0:T(8,128)S(1)} %squeeze.98), channel_id=1, source_target_pairs={{0,32},{4,36},{8,40},{12,44},{16,48},{20,52},{24,56},{28,60},{32,6... | collective-permute-start | bytes 36872 | tf_op jit(solution)/shard_map/ppermute | solution.py:12
  201.1 417.3 %psum.33 = f32[16]{0:T(128)} all-reduce(f32[16]{0:T(128)S(1)} %add.136), channel_id=1, replica_groups=mesh['sub'=128,'scen'=4] {'sub'}, use_global_device_ids=true, to_apply=%region_10.11 | all-reduce | flops 16 | bytes 128 | tf_op jit(solution)/shard_map/psum | solution.py:124
  618.5 10.8 %psum.32 = f32[16]{0:T(128)} all-reduce(f32[16]{0:T(128)S(1)} %add.135), channel_id=1, replica_groups=mesh['sub'=128,'scen'=4] {'scen'}, use_global_device_ids=true, to_apply=%region_5.6 | all-reduce | flops 16 | bytes 128 | tf_op jit(solution)/shard_map/psum | solution.py:123
  (262 shorter events, 107.5 us)
Async XLA Ops:
  3.6 5.6 copy-start.24
  6.0 2.5 copy-start.20
  8.4 2.8 copy-start.29
  9.2 49.7 %copy-start.11 = (pred[1024,32]{0,1:T(8,128)(4,1)}, pred[1024,32]{0,1:T(8,128)(4,1)S(1)}, u32[]{:S(2)}) copy-start(pred[1024,32]{0,1:T(8,128)(4,1)S(1)} %iota_compare_fusion.5) | copy-start | bytes 98308
  9.2 3.4 copy-start.26
  9.2 3.4 copy-start
  9.2 3.4 copy-start.3
  9.2 3.4 copy-start.9
  12.6 46.2 %copy-start.28 = (s32[1,16]{1,0:T(1,128)S(1)}, s32[1,16]{1,0:T(1,128)}, u32[]{:S(2)}) copy-start(s32[1,16]{1,0:T(1,128)} %param.27) | copy-start | bytes 196
  61.8 29.5 %copy-start.8 = (f32[1,48,16,16]{1,3,2,0:T(8,128)S(1)}, f32[1,48,16,16]{1,3,2,0:T(8,128)}, u32[]{:S(2)}) copy-start(f32[1,48,16,16]{1,3,2,0:T(8,128)} %param.28) | copy-start | bytes 147460
  61.8 30.2 %copy-start.21 = (f32[48,16]{0,1:T(8,128)S(1)}, f32[48,16]{0,1:T(8,128)}, u32[]{:S(2)}) copy-start(f32[48,16]{0,1:T(8,128)} %param.31) | copy-start | bytes 9220
  62.0 30.1 %copy-start.22 = (f32[24,16]{0,1:T(8,128)S(1)}, f32[24,16]{0,1:T(8,128)}, u32[]{:S(2)}) copy-start(f32[24,16]{0,1:T(8,128)} %get-tuple-element.466) | copy-start | bytes 4612
  63.5 33.2 %collective-permute-start = (f32[8,384]{1,0:T(8,128)}, f32[8,384]{1,0:T(8,128)S(1)}, u32[]{:S(2)}, u32[]{:S(2)}) collective-permute-start(f32[8,384]{1,0:T(8,128)} %squeeze.91), channel_id=1, source_target_pairs={{0,508},{4,0},{8,4},{12,8},{16,12},{20,16},{24,20},{28,24},{32,28}... | collective-permute-start | bytes 36872 | tf_op jit(solution)/shard_map/ppermute | solution.py:12
  78.1 18.7 %collective-permute-start.1 = (f32[8,384]{1,0:T(8,128)S(1)}, f32[8,384]{1,0:T(8,128)S(1)}, u32[]{:S(2)}, u32[]{:S(2)}) collective-permute-start(f32[8,384]{1,0:T(8,128)S(1)} %squeeze.92), channel_id=1, source_target_pairs={{0,4},{4,8},{8,12},{12,16},{16,20},{20,24},{24,28},{28,32},{32,36}... | collective-permute-start | bytes 36872 | tf_op jit(solution)/shard_map/ppermute | solution.py:12
  80.8 16.3 %collective-permute-start.2 = (f32[8,384]{1,0:T(8,128)}, f32[8,384]{1,0:T(8,128)}, u32[]{:S(2)}, u32[]{:S(2)}) collective-permute-start(f32[8,384]{1,0:T(8,128)} %squeeze.93), channel_id=1, source_target_pairs={{0,480},{4,484},{8,488},{12,492},{16,496},{20,500},{24,504},{28,50... | collective-permute-start | bytes 36872 | tf_op jit(solution)/shard_map/ppermute | solution.py:12
  86.2 16.5 %collective-permute-start.3 = (f32[8,384]{1,0:T(8,128)S(1)}, f32[8,384]{1,0:T(8,128)}, u32[]{:S(2)}, u32[]{:S(2)}) collective-permute-start(f32[8,384]{1,0:T(8,128)S(1)} %squeeze.94), channel_id=1, source_target_pairs={{0,32},{4,36},{8,40},{12,44},{16,48},{20,52},{24,56},{28,60},{32,6... | collective-permute-start | bytes 36872 | tf_op jit(solution)/shard_map/ppermute | solution.py:12
  95.1 10.2 %copy-start.25 = (s32[32]{0:T(128)S(1)}, s32[32]{0:T(128)}, u32[]{:S(2)}) copy-start(s32[32]{0:T(128)} %copy-done.24) | copy-start | bytes 388
  95.1 10.2 %copy-start.27 = (f32[32]{0:T(128)S(1)}, f32[32]{0:T(128)}, u32[]{:S(2)}) copy-start(f32[32]{0:T(128)} %copy-done.26) | copy-start | bytes 388
  97.9 7.2 %copy-start.4 = (f32[1,8,24,16]{2,3,1,0:T(8,128)}, f32[1,8,24,16]{2,3,1,0:T(8,128)S(1)}, u32[]{:S(2)}) copy-start(f32[1,8,24,16]{2,3,1,0:T(8,128)S(1)} %copy.48) | copy-start | bytes 36868
  108.7 62.3 %copy-start.13 = (f32[16,1024]{1,0:T(8,128)S(1)}, f32[16,1024]{1,0:T(8,128)}, u32[]{:S(2)}) copy-start(f32[16,1024]{1,0:T(8,128)} %fusion.55) | copy-start | bytes 196612
  171.0 2.4 copy-start.1
  171.0 2.4 copy-start.12
  174.3 25.9 %copy-start.16 = (f32[384,16]{0,1:T(8,128)S(1)}, f32[384,16]{0,1:T(8,128)}, u32[]{:S(2)}) copy-start(f32[384,16]{0,1:T(8,128)} %squeeze.100) | copy-start | bytes 73732
  174.3 25.9 %copy-start.17 = (f32[384,16]{0,1:T(8,128)S(1)}, f32[384,16]{0,1:T(8,128)}, u32[]{:S(2)}) copy-start(f32[384,16]{0,1:T(8,128)} %squeeze.99) | copy-start | bytes 73732
  174.3 26.8 %copy-start.18 = (f32[24,16]{1,0:T(8,128)S(1)}, f32[24,16]{1,0:T(8,128)}, u32[]{:S(2)}) copy-start(f32[24,16]{1,0:T(8,128)} %copy.62) | copy-start | bytes 4612
  174.3 26.8 %copy-start.19 = (f32[24,16]{1,0:T(8,128)S(1)}, f32[24,16]{1,0:T(8,128)}, u32[]{:S(2)}) copy-start(f32[24,16]{1,0:T(8,128)} %copy.63) | copy-start | bytes 4612
  174.5 455.5 %copy-start.5 = (f32[1,8,24,16]{2,3,1,0:T(8,128)S(1)}, f32[1,8,24,16]{2,3,1,0:T(8,128)}, u32[]{:S(2)}) copy-start(f32[1,8,24,16]{2,3,1,0:T(8,128)} %copy-done.4) | copy-start | bytes 36868
  174.5 455.5 %copy-start.7 = (f32[1,8,24,16]{2,3,1,0:T(8,128)S(1)}, f32[1,8,24,16]{2,3,1,0:T(8,128)}, u32[]{:S(2)}) copy-start(f32[1,8,24,16]{2,3,1,0:T(8,128)} %copy-done.6) | copy-start | bytes 36868
  174.8 454.5 %collective-permute-start.4 = (f32[8,384]{1,0:T(8,128)S(1)}, f32[8,384]{1,0:T(8,128)S(1)}, u32[]{:S(2)}, u32[]{:S(2)}) collective-permute-start(f32[8,384]{1,0:T(8,128)S(1)} %squeeze.95), channel_id=1, source_target_pairs={{0,508},{4,0},{8,4},{12,8},{16,12},{20,16},{24,20},{28,24},{32,28}... | collective-permute-start | bytes 36872 | tf_op jit(solution)/shard_map/ppermute | solution.py:12
  188.3 441.1 %collective-permute-start.5 = (f32[8,384]{1,0:T(8,128)S(1)}, f32[8,384]{1,0:T(8,128)S(1)}, u32[]{:S(2)}, u32[]{:S(2)}) collective-permute-start(f32[8,384]{1,0:T(8,128)S(1)} %squeeze.96), channel_id=1, source_target_pairs={{0,4},{4,8},{8,12},{12,16},{16,20},{20,24},{24,28},{28,32},{32,36}... | collective-permute-start | bytes 36872 | tf_op jit(solution)/shard_map/ppermute | solution.py:12
  190.3 439.3 %collective-permute-start.6 = (f32[8,384]{1,0:T(8,128)S(1)}, f32[8,384]{1,0:T(8,128)S(1)}, u32[]{:S(2)}, u32[]{:S(2)}) collective-permute-start(f32[8,384]{1,0:T(8,128)S(1)} %squeeze.97), channel_id=1, source_target_pairs={{0,480},{4,484},{8,488},{12,492},{16,496},{20,500},{24,504},{28,50... | collective-permute-start | bytes 36872 | tf_op jit(solution)/shard_map/ppermute | solution.py:12
  192.3 437.4 %collective-permute-start.7 = (f32[8,384]{1,0:T(8,128)S(1)}, f32[8,384]{1,0:T(8,128)S(1)}, u32[]{:S(2)}, u32[]{:S(2)}) collective-permute-start(f32[8,384]{1,0:T(8,128)S(1)} %squeeze.98), channel_id=1, source_target_pairs={{0,32},{4,36},{8,40},{12,44},{16,48},{20,52},{24,56},{28,60},{32,6... | collective-permute-start | bytes 36872 | tf_op jit(solution)/shard_map/ppermute | solution.py:12
  (6 other events, 10.4 us)
where the time goes:
time: 635 us; the launch traced here: 631 us
  blocking collectives  428 us (67%)
  matrix products  102 us (16%)
  starting transfers between devices  51.3 us (8%)
  local copies, waits for them, and re-layouts  35.8 us (6%)
  other arithmetic  7.83 us (1%)
    psum x1, blocking collectives, body(): fault_local = fault_local + lax.psum(fault_term, 'sub')  417 us
    dot_general x48, matrix products, one_step(): jnp.dot(right_side.astype(jnp.bfloat16), weights, preferred_element_type=...  91.4 us
    ppermute x8, starting transfers between devices, passed_along(): return lax.ppermute(value, axis, pairs)  51.3 us
    mul x48, local copies, waits for them, and re-layouts, one_step(): current_now[:, None] * fault_table  16.6 us
  transfers between devices with their start and end apart: 8, of which 1 were waited for; matrix products, arithmetic and copies ran while one was open for 2% of the time, Pallas kernels for 0%

commit v1 on v0

--- a/solution.py
+++ b/solution.py
@@ -121,7 +121,7 @@
             axis=0,
         )
         control_local = control_local + lax.psum(control_term, "scen")
-        fault_local = fault_local + lax.psum(fault_term, "sub")
+        fault_local = fault_local + jnp.sum(lax.all_gather(fault_term, "sub"), axis=0)
         received = jnp.stack(
             [
                 passed_along(outbound[opposite[direction]], "sub", -offsets[direction])

time: 635 us -> 1040 us (1.64)
  blocking collectives: 428 us -> 827 us
    unnamed x0 -> x1, blocking collectives: none -> 815 us
    psum x1 -> x0, blocking collectives: 417 us -> none  [body(): fault_local = fault_local + lax.psum(fault_term, 'sub')]
  transfers between devices with their start and end apart: 8 -> 8, of which waited for: 1 -> 1; matrix products, arithmetic and copies ran while one was open for 2% -> 1% of each run, Pallas kernels for 0% -> 0%
where the time goes in v1:
time: 1040 us; the launch traced here: 1030 us
  blocking collectives  827 us (80%)
  matrix products  101 us (10%)
  starting transfers between devices  53.2 us (5%)
  local copies, waits for them, and re-layouts  37.7 us (4%)
    unnamed x1, blocking collectives  815 us
    dot_general x48, matrix products, one_step(): jnp.dot(right_side.astype(jnp.bfloat16), weights, preferred_element_type=...  91 us
    ppermute x8, starting transfers between devices, passed_along(): return lax.ppermute(value, axis, pairs)  53.2 us
  transfers between devices with their start and end apart: 8, of which 1 were waited for; matrix products, arithmetic and copies ran while one was open for 1% of the time, Pallas kernels for 0%

profile of v1, /device:TPU:64, one launch (start us, length us, event | category | flops | bytes accessed | tf_op | source)
XLA Modules:
  0.0 1032.2 jit_solution(126828645566387175)
XLA Ops:
  5.9 2.4 slice_bitcast_fusion
  9.2 2.0 fusion.45
  12.6 45.9 %while.34 = (s32[]{:T(128)}, f32[16,1024]{1,0:T(8,128)S(1)}, f32[24,16,1024]{2,1,0:T(8,128)}, bf16[24,16,1024]{2,1,0:T(8,128)(2,1)}, f32[1,1024]{1,0:T(1,128)S(1...) while((s32[]{:T(128)}, f32[16,1024]{1,0:T(8,128)S(1)}, ...), condition=%wide.region_1.2_spmd.clone, body=%wide.region_0.1_spmd.clone.sunk | while | flops 33685504 | bytes 2528637 | solution.py:93
  14.5 1.9 bitcast_dynamic-update-slice_fusion.4
  18.3 1.9 bitcast_dynamic-update-slice_fusion.4
  20.3 1.9 bitcast_dynamic-update-slice_fusion.4
  22.2 1.9 bitcast_dynamic-update-slice_fusion.4
  26.0 1.9 bitcast_dynamic-update-slice_fusion.4
  31.7 1.9 bitcast_dynamic-update-slice_fusion.4
  39.4 1.9 bitcast_dynamic-update-slice_fusion.4
  43.2 1.9 bitcast_dynamic-update-slice_fusion.4
  47.0 1.9 bitcast_dynamic-update-slice_fusion.4
  52.8 1.9 bitcast_dynamic-update-slice_fusion.4
  54.7 1.9 bitcast_dynamic-update-slice_fusion.4
  56.6 1.9 bitcast_dynamic-update-slice_fusion.4
  58.6 2.3 fusion.57
  63.2 14.5 %collective-permute-start = (f32[8,384]{1,0:T(8,128)}, f32[8,384]{1,0:T(8,128)S(1)}, u32[]{:S(2)}, u32[]{:S(2)}) collective-permute-start(f32[8,384]{1,0:T(8,128)} %squeeze.91), channel_id=1, source_target_pairs={{0,508},{4,0},{8,4},{12,8},{16,12},{20,16},{24,20},{28,24},{32,28}... | collective-permute-start | bytes 36872 | tf_op jit(solution)/shard_map/ppermute | solution.py:12
  77.9 1.9 collective-permute-start.1
  80.5 5.3 collective-permute-start.2
  85.9 4.4 collective-permute-start.3
  99.6 2.8 collective-permute-done.3
  105.1 2.0 fusion.43
  108.4 62.1 %while.35 = (s32[]{:T(128)}, f32[16,1024]{1,0:T(8,128)S(1)}, f32[24,16,1024]{2,1,0:T(8,128)}, bf16[24,16,1024]{2,1,0:T(8,128)(2,1)S(1)}, f32[1,1024]{1,0:T(1,128...) while((s32[]{:T(128)}, f32[16,1024]{1,0:T(8,128)S(1)}, ...), condition=%wide.region_3.4_spmd.clone, body=%wide.region_2.3_spmd.clone.sunk | while | flops 33685504 | bytes 2529533 | solution.py:93
  142.7 1.9 bitcast_dynamic-update-slice_fusion.5
  158.2 1.9 bitcast_dynamic-update-slice_fusion.5
  170.5 2.3 multiply_reduce_fusion
  174.3 15.4 %collective-permute-start.4 = (f32[8,384]{1,0:T(8,128)S(1)}, f32[8,384]{1,0:T(8,128)S(1)}, u32[]{:S(2)}, u32[]{:S(2)}) collective-permute-start(f32[8,384]{1,0:T(8,128)S(1)} %squeeze.95), channel_id=1, source_target_pairs={{0,508},{4,0},{8,4},{12,8},{16,12},{20,16},{24,20},{28,24},{32,28}... | collective-permute-start | bytes 36872 | tf_op jit(solution)/shard_map/ppermute | solution.py:12
  189.7 1.9 collective-permute-start.5
  191.8 1.9 collective-permute-start.6
  193.8 7.8 collective-permute-start.7
  203.1 814.6 %all-reduce.2 = (f32[2048]{0:T(1024)S(1)}, f32[2048]{0:T(1024)S(1)}) all-reduce(f32[2048]{0:T(1024)S(1)} %dynamic-update-slice, f32[2048]{0:T(1024)S(1)} %dynamic-update-slice.1), channel_id=2, replica_groups=mesh['sub'=128,'scen'=4] {'sub'}, use_global_device_ids=true, to_apply=%add | all-reduce | flops 4096 | bytes 32768
  1018.4 12.2 %psum.16 = f32[16]{0:T(128)} all-reduce(f32[16]{0:T(128)S(1)} %add.131), channel_id=1, replica_groups=mesh['sub'=128,'scen'=4] {'scen'}, use_global_device_ids=true, to_apply=%region_5.6 | all-reduce | flops 16 | bytes 128 | tf_op jit(solution)/shard_map/psum | solution.py:123
  (271 shorter events, 109.7 us)
Async XLA Ops:
  3.5 5.6 copy-start.24
  5.9 2.4 copy-start.20
  8.4 2.8 copy-start.29
  9.1 49.5 %copy-start.11 = (pred[1024,32]{0,1:T(8,128)(4,1)}, pred[1024,32]{0,1:T(8,128)(4,1)S(1)}, u32[]{:S(2)}) copy-start(pred[1024,32]{0,1:T(8,128)(4,1)S(1)} %iota_compare_fusion.5) | copy-start | bytes 98308
  9.2 3.4 copy-start.26
  9.2 3.4 copy-start
  9.2 3.4 copy-start.3
  9.2 3.3 copy-start.9
  12.5 45.9 %copy-start.28 = (s32[1,16]{1,0:T(1,128)S(1)}, s32[1,16]{1,0:T(1,128)}, u32[]{:S(2)}) copy-start(s32[1,16]{1,0:T(1,128)} %param.27) | copy-start | bytes 196
  61.5 29.5 %copy-start.8 = (f32[1,48,16,16]{1,3,2,0:T(8,128)S(1)}, f32[1,48,16,16]{1,3,2,0:T(8,128)}, u32[]{:S(2)}) copy-start(f32[1,48,16,16]{1,3,2,0:T(8,128)} %param.28) | copy-start | bytes 147460
  61.5 30.2 %copy-start.21 = (f32[48,16]{0,1:T(8,128)S(1)}, f32[48,16]{0,1:T(8,128)}, u32[]{:S(2)}) copy-start(f32[48,16]{0,1:T(8,128)} %param.31) | copy-start | bytes 9220
  61.7 30.1 %copy-start.22 = (f32[24,16]{0,1:T(8,128)S(1)}, f32[24,16]{0,1:T(8,128)}, u32[]{:S(2)}) copy-start(f32[24,16]{0,1:T(8,128)} %get-tuple-element.468) | copy-start | bytes 4612
  63.2 35.1 %collective-permute-start = (f32[8,384]{1,0:T(8,128)}, f32[8,384]{1,0:T(8,128)S(1)}, u32[]{:S(2)}, u32[]{:S(2)}) collective-permute-start(f32[8,384]{1,0:T(8,128)} %squeeze.91), channel_id=1, source_target_pairs={{0,508},{4,0},{8,4},{12,8},{16,12},{20,16},{24,20},{28,24},{32,28}... | collective-permute-start | bytes 36872 | tf_op jit(solution)/shard_map/ppermute | solution.py:12
  77.9 20.7 %collective-permute-start.1 = (f32[8,384]{1,0:T(8,128)S(1)}, f32[8,384]{1,0:T(8,128)S(1)}, u32[]{:S(2)}, u32[]{:S(2)}) collective-permute-start(f32[8,384]{1,0:T(8,128)S(1)} %squeeze.92), channel_id=1, source_target_pairs={{0,4},{4,8},{8,12},{12,16},{16,20},{20,24},{24,28},{28,32},{32,36}... | collective-permute-start | bytes 36872 | tf_op jit(solution)/shard_map/ppermute | solution.py:12
  80.5 18.2 %collective-permute-start.2 = (f32[8,384]{1,0:T(8,128)}, f32[8,384]{1,0:T(8,128)}, u32[]{:S(2)}, u32[]{:S(2)}) collective-permute-start(f32[8,384]{1,0:T(8,128)} %squeeze.93), channel_id=1, source_target_pairs={{0,480},{4,484},{8,488},{12,492},{16,496},{20,500},{24,504},{28,50... | collective-permute-start | bytes 36872 | tf_op jit(solution)/shard_map/ppermute | solution.py:12
  85.9 16.5 %collective-permute-start.3 = (f32[8,384]{1,0:T(8,128)S(1)}, f32[8,384]{1,0:T(8,128)}, u32[]{:S(2)}, u32[]{:S(2)}) collective-permute-start(f32[8,384]{1,0:T(8,128)S(1)} %squeeze.94), channel_id=1, source_target_pairs={{0,32},{4,36},{8,40},{12,44},{16,48},{20,52},{24,56},{28,60},{32,6... | collective-permute-start | bytes 36872 | tf_op jit(solution)/shard_map/ppermute | solution.py:12
  94.8 10.2 copy-start.25
  94.9 10.2 copy-start.27
  99.6 5.2 copy-start.4
  108.4 62.1 %copy-start.13 = (f32[16,1024]{1,0:T(8,128)S(1)}, f32[16,1024]{1,0:T(8,128)}, u32[]{:S(2)}) copy-start(f32[16,1024]{1,0:T(8,128)} %fusion.55) | copy-start | bytes 196612
  170.5 2.4 copy-start.1
  170.5 2.4 copy-start.12
  173.8 27.9 %copy-start.16 = (f32[384,16]{0,1:T(8,128)S(1)}, f32[384,16]{0,1:T(8,128)}, u32[]{:S(2)}) copy-start(f32[384,16]{0,1:T(8,128)} %squeeze.100) | copy-start | bytes 73732
  173.8 27.9 %copy-start.17 = (f32[384,16]{0,1:T(8,128)S(1)}, f32[384,16]{0,1:T(8,128)}, u32[]{:S(2)}) copy-start(f32[384,16]{0,1:T(8,128)} %squeeze.99) | copy-start | bytes 73732
  173.8 28.7 %copy-start.18 = (f32[24,16]{1,0:T(8,128)S(1)}, f32[24,16]{1,0:T(8,128)}, u32[]{:S(2)}) copy-start(f32[24,16]{1,0:T(8,128)} %copy.62) | copy-start | bytes 4612
  173.8 28.7 %copy-start.19 = (f32[24,16]{1,0:T(8,128)S(1)}, f32[24,16]{1,0:T(8,128)}, u32[]{:S(2)}) copy-start(f32[24,16]{1,0:T(8,128)} %copy.63) | copy-start | bytes 4612
  174.1 857.2 %copy-start.5 = (f32[1,8,24,16]{2,3,1,0:T(8,128)S(1)}, f32[1,8,24,16]{2,3,1,0:T(8,128)}, u32[]{:S(2)}) copy-start(f32[1,8,24,16]{2,3,1,0:T(8,128)} %copy-done.4) | copy-start | bytes 36868
  174.1 857.2 %copy-start.7 = (f32[1,8,24,16]{2,3,1,0:T(8,128)S(1)}, f32[1,8,24,16]{2,3,1,0:T(8,128)}, u32[]{:S(2)}) copy-start(f32[1,8,24,16]{2,3,1,0:T(8,128)} %copy-done.6) | copy-start | bytes 36868
  174.3 856.3 %collective-permute-start.4 = (f32[8,384]{1,0:T(8,128)S(1)}, f32[8,384]{1,0:T(8,128)S(1)}, u32[]{:S(2)}, u32[]{:S(2)}) collective-permute-start(f32[8,384]{1,0:T(8,128)S(1)} %squeeze.95), channel_id=1, source_target_pairs={{0,508},{4,0},{8,4},{12,8},{16,12},{20,16},{24,20},{28,24},{32,28}... | collective-permute-start | bytes 36872 | tf_op jit(solution)/shard_map/ppermute | solution.py:12
  189.7 841.0 %collective-permute-start.5 = (f32[8,384]{1,0:T(8,128)S(1)}, f32[8,384]{1,0:T(8,128)S(1)}, u32[]{:S(2)}, u32[]{:S(2)}) collective-permute-start(f32[8,384]{1,0:T(8,128)S(1)} %squeeze.96), channel_id=1, source_target_pairs={{0,4},{4,8},{8,12},{12,16},{16,20},{20,24},{24,28},{28,32},{32,36}... | collective-permute-start | bytes 36872 | tf_op jit(solution)/shard_map/ppermute | solution.py:12
  191.8 839.2 %collective-permute-start.6 = (f32[8,384]{1,0:T(8,128)S(1)}, f32[8,384]{1,0:T(8,128)S(1)}, u32[]{:S(2)}, u32[]{:S(2)}) collective-permute-start(f32[8,384]{1,0:T(8,128)S(1)} %squeeze.97), channel_id=1, source_target_pairs={{0,480},{4,484},{8,488},{12,492},{16,496},{20,500},{24,504},{28,50... | collective-permute-start | bytes 36872 | tf_op jit(solution)/shard_map/ppermute | solution.py:12
  193.8 837.4 %collective-permute-start.7 = (f32[8,384]{1,0:T(8,128)S(1)}, f32[8,384]{1,0:T(8,128)S(1)}, u32[]{:S(2)}, u32[]{:S(2)}) collective-permute-start(f32[8,384]{1,0:T(8,128)S(1)} %squeeze.98), channel_id=1, source_target_pairs={{0,32},{4,36},{8,40},{12,44},{16,48},{20,52},{24,56},{28,60},{32,6... | collective-permute-start | bytes 36872 | tf_op jit(solution)/shard_map/ppermute | solution.py:12
  (6 other events, 10.4 us)
